TPU v7x, 128 devices: a whole 4x4x4 slice. The times are simulated.
128 devices in a mesh: group: 4 (over x), expert: 32 (over y, z, core).
Axes of the slice: x: 4, y: 4, z: 4, core: 2. Of those that a mesh axis runs over, the one named last changes fastest.
Arguments:
- tokens: bfloat16 [16384, 2048], P(('group', 'expert')), may hold values from -6 to 6
- cotangent: bfloat16 [16384, 2048], P(('group', 'expert')), may hold values from -6 to 6
- gate_probs: float32 [16384, 8], P(('group', 'expert')), may hold values from 0.02 to 0.5
- expert_ids: int32 [16384, 8], P(('group', 'expert')), may hold values from 0 to 31, all different within a row; in each aligned block of 128 rows (0 to 127, 128 to 255, ...) at most 72 rows name the same one
- gate_up: bfloat16 [32, 2048, 768], P('expert'), may hold values from -0.125 to 0.125
- down_weight: bfloat16 [32, 384, 2048], P('expert'), may hold values from -0.3125 to 0.3125
- gate_up_moment: float32 [32, 2048, 768], P('expert', 'group'), may hold values from -6 to 6
- gate_up_second: float32 [32, 2048, 768], P('expert', 'group'), may hold values from 0.05 to 20
- down_moment: float32 [32, 384, 2048], P('expert', None, 'group'), may hold values from -6 to 6
- down_second: float32 [32, 384, 2048], P('expert', None, 'group'), may hold values from 0.05 to 20
Outputs:
- token_grad: bfloat16 [16384, 2048], P(('group', 'expert'))
- updated_gate_up: bfloat16 [32, 2048, 768], P('expert')
- updated_down: bfloat16 [32, 384, 2048], P('expert')
- gate_up_moment_out: float32 [32, 2048, 768], P('expert', 'group')
- gate_up_second_out: float32 [32, 2048, 768], P('expert', 'group')
- down_moment_out: float32 [32, 384, 2048], P('expert', None, 'group')
- down_second_out: float32 [32, 384, 2048], P('expert', None, 'group')
Inputs may be any that keep to these rules, and one draw needn't show every extreme that they name: `expert_ids`: each row names 8 different experts. In the rows of one device no expert is named by more than 72 rows, and in every draw some expert is named by exactly 72 rows of some device.
All inputs are finite; a program needn't handle non-finite values.
Results may differ from a plain program's by a relative error of at most 0.015.
Values may be sent and summed in bfloat16 or wider, within the bound.
No kernel may reach another device: no remote copies, remote signals or barrier semaphores. Data moves between devices by JAX's collectives and lax.ppermute only.
A program may use at most 192 MiB of HBM per device.

v0:
```python
import jax
import jax.numpy as jnp
from jax import lax
from jax.sharding import PartitionSpec as P

learn_rate = 0.001
beta_first = 0.9
beta_second = 0.999
adam_eps = 1e-08


def expert_backward(inputs, scaled_parts, weight_gate_up, weight_down):
    hidden_count = weight_down.shape[0]
    width = scaled_parts[0].shape[1]
    projected = jnp.dot(inputs, weight_gate_up, preferred_element_type=jnp.float32)
    gate_part = projected[:, :hidden_count]
    up_part = projected[:, hidden_count:]
    sigmoid_gate = jax.nn.sigmoid(gate_part)
    activated = gate_part * sigmoid_gate
    hidden_act = (activated * up_part).astype(jnp.bfloat16)
    hidden_grad = sum(
        (
            jnp.dot(
                part,
                weight_down[:, i * width : (i + 1) * width].T,
                preferred_element_type=jnp.float32,
            )
            for i, part in enumerate(scaled_parts)
        )
    )
    slope = sigmoid_gate * (1.0 + gate_part * (1.0 - sigmoid_gate))
    hidden_act, up_slope, activated = lax.optimization_barrier(
        (hidden_act, up_part * slope, activated)
    )
    pair_grad = jnp.concatenate([hidden_grad * up_slope, hidden_grad * activated], axis=1).astype(
        jnp.bfloat16
    )
    down_grad = jnp.dot(
        hidden_act.T, jnp.concatenate(scaled_parts, axis=1), preferred_element_type=jnp.float32
    )
    gate_up_grad = jnp.dot(inputs.T, pair_grad, preferred_element_type=jnp.float32)
    input_grad = jnp.dot(pair_grad, weight_gate_up.T, preferred_element_type=jnp.float32).astype(
        jnp.bfloat16
    )
    return (gate_up_grad, down_grad, input_grad)


def adam_update(weight, grad, first, second):
    first_new = beta_first * first + (1.0 - beta_first) * grad
    second_new = beta_second * second + (1.0 - beta_second) * grad * grad
    updated = (
        weight.astype(jnp.float32) - learn_rate * first_new / (jnp.sqrt(second_new) + adam_eps)
    ).astype(jnp.bfloat16)
    return (updated, first_new, second_new)


def exclusive_count(flags):
    n = flags.shape[-1]
    earlier = (jnp.arange(n)[:, None] < jnp.arange(n)[None, :]).astype(jnp.bfloat16)
    return jnp.dot(flags.astype(jnp.bfloat16), earlier, preferred_element_type=jnp.float32)


def local(
    tokens,
    cotangent,
    gate_probs,
    expert_ids,
    gate_up,
    down_weight,
    gate_up_moment,
    gate_up_second,
    down_moment,
    down_second,
):
    expert_count = lax.axis_size("expert")
    me = lax.axis_index("expert")
    local_tokens, model_width = tokens.shape
    top_count = expert_ids.shape[1]
    capacity = min(local_tokens, 9 * local_tokens * top_count // (4 * expert_count))
    slot_total = expert_count * capacity
    half_width = model_width // 2
    pieces = []
    rest = gate_probs
    for _ in range(3):
        piece = lax.reduce_precision(rest, exponent_bits=8, mantissa_bits=7)
        pieces.append(piece)
        rest = rest - piece
    meta = jnp.concatenate([expert_ids.astype(jnp.float32)] + pieces, axis=1)
    meta_width = 128
    meta = jnp.pad(meta, ((0, 0), (0, meta_width - meta.shape[1]))).astype(jnp.bfloat16)
    first = lax.all_gather(
        jnp.concatenate([tokens, cotangent[:, :half_width], meta], axis=1), "expert", axis=0
    )
    first, cot_after = lax.optimization_barrier((first, cotangent))
    cot_hi = lax.all_gather(cot_after[:, half_width:], "expert", axis=0)
    meta_at = model_width + half_width
    all_meta = first[..., meta_at : meta_at + 4 * top_count].astype(jnp.float32)
    all_ids = all_meta[..., :top_count].astype(jnp.int32)
    all_gates = (
        all_meta[..., top_count : 2 * top_count]
        + all_meta[..., 2 * top_count : 3 * top_count]
        + all_meta[..., 3 * top_count :]
    )
    match = all_ids == me
    routed = jnp.any(match, axis=-1).astype(jnp.float32)
    gate_of = jnp.sum(jnp.where(match, all_gates, 0.0), axis=-1)
    rank = exclusive_count(routed)
    slots = jnp.arange(capacity, dtype=jnp.float32)
    pick = (routed[:, None, :] > 0) & (rank[:, None, :] == slots[None, :, None])
    pick_b = pick.astype(jnp.bfloat16)
    picked_first = jnp.einsum(
        "srt,stc->src", pick_b, first, preferred_element_type=jnp.float32
    ).astype(jnp.bfloat16)
    inputs = picked_first[..., :model_width]
    slot_gate = jnp.sum(jnp.where(pick, gate_of[:, None, :], 0.0), axis=-1)
    picked_hi = jnp.einsum(
        "srt,stc->src", pick_b, cot_hi, preferred_element_type=jnp.float32
    ).astype(jnp.bfloat16)
    scaled = [
        (slot_gate[..., None] * part.astype(jnp.float32))
        .astype(jnp.bfloat16)
        .reshape(slot_total, half_width)
        for part in (picked_first[..., model_width:meta_at], picked_hi)
    ]
    weight_pair = gate_up[0]
    weight_down = down_weight[0]
    grad_pair, grad_down, row_grads = expert_backward(
        inputs.reshape(slot_total, model_width), scaled, weight_pair, weight_down
    )
    dense = jnp.einsum(
        "srt,src->stc",
        pick_b,
        row_grads.reshape(expert_count, capacity, model_width),
        preferred_element_type=jnp.float32,
    ).astype(jnp.bfloat16)
    token_grad = lax.psum_scatter(
        dense.reshape(expert_count * local_tokens, model_width),
        "expert",
        scatter_dimension=0,
        tiled=True,
    )
    groups = lax.axis_size("group")
    share_rows = model_width // groups
    hidden_count = grad_down.shape[0]
    pair_width = grad_pair.shape[1]
    pair_parts = lax.all_to_all(
        grad_pair.astype(jnp.bfloat16).reshape(groups, share_rows, pair_width),
        "group",
        0,
        0,
        tiled=True,
    )
    down_parts = lax.all_to_all(
        grad_down.astype(jnp.bfloat16).reshape(hidden_count, groups, share_rows),
        "group",
        1,
        1,
        tiled=True,
    )
    sum_pair = jnp.sum(pair_parts.astype(jnp.float32), axis=0)[None]
    sum_down = jnp.sum(down_parts.astype(jnp.float32), axis=1)[None]
    token_grad, sum_down = lax.optimization_barrier((token_grad, sum_down))
    group_index = lax.axis_index("group")
    own_pair = lax.dynamic_slice_in_dim(gate_up, group_index * share_rows, share_rows, 1)
    own_down = lax.dynamic_slice_in_dim(down_weight, group_index * share_rows, share_rows, 2)
    new_pair, first_pair, second_pair = adam_update(
        own_pair, sum_pair, gate_up_moment, gate_up_second
    )
    new_down, first_down, second_down = adam_update(own_down, sum_down, down_moment, down_second)
    full_pair = lax.all_to_all(
        jnp.broadcast_to(new_pair, (groups, share_rows, pair_width)), "group", 0, 0, tiled=True
    ).reshape(1, model_width, pair_width)
    full_down = lax.all_gather(new_down, "group", axis=2, tiled=True)
    return (token_grad, full_pair, full_down, first_pair, second_pair, first_down, second_down)


def solution(mesh):
    rows = P(("group", "expert"), None)
    placed = (
        rows,
        rows,
        rows,
        rows,
        P("expert", None, None),
        P("expert", None, None),
        P("expert", "group", None),
        P("expert", "group", None),
        P("expert", None, "group"),
        P("expert", None, "group"),
    )
    return jax.shard_map(
        local,
        mesh=mesh,
        in_specs=placed,
        out_specs=(
            rows,
            P("expert", None, None),
            P("expert", None, None),
            P("expert", "group", None),
            P("expert", "group", None),
            P("expert", None, "group"),
            P("expert", None, "group"),
        ),
        check_vma=False,
    )
```

profile of v0, /device:TPU:1, one launch (start us, length us, event | category | flops | bytes accessed | tf_op | source)
XLA Modules:
  0.0 347.5 jit_solution(9185191989546034513)
XLA Ops:
  11.8 98.6 %all-gather.8.cloned.1.call-done = bf16[4096,3200]{1,0:T(8,128)(2,1)} async-done(((bf16[128,3200]{1,0:T(8,128)(2,1)}), bf16[4096,3200]{1,0:T(8,128)(2,1)}) %all-gather.8.cloned.1.call-update) | async-done | bytes 26214416 | tf_op jit(solution)/shard_map/all_gather | solution.py:91
  112.7 3.0 fusion.12
  116.9 15.9 %convolution_convert_fusion.1 = bf16[32,72,3200]{2,1,0:T(8,128)(2,1)} fusion(bf16[32,128,3200]{2,1,0:T(8,128)(2,1)} %bitcast.41, f32[32,128]{1,0:T(8,128)S(1)} %fusion.33, pred[32,128]{1,0:T(8,128)(4,1)S(1)} %convert_compare_fusion), kind=kOutput, calls=%fused_computation.1 | convolution fusion | flops 1895399424 | bytes 40980480 | tf_op jit(solution)/shard_map/srt,stc->src/dot_general | solution.py:111
  132.8 9.4 %slice.59 = bf16[32,72,2048]{2,1,0:T(8,128)(2,1)} slice(bf16[32,72,3200]{2,1,0:T(8,128)(2,1)} %convolution_convert_fusion.1), slice={[0:32], [0:72], [0:2048]} | slice | bytes 18874368 | tf_op jit(solution)/shard_map/slice | solution.py:114
  142.3 10.6 %fusion.6 = f32[2304,768]{0,1:T(8,128)S(1)} fusion(bf16[2304,2048]{1,0:T(8,128)(2,1)} %bitcast.44, bf16[1,2048,768]{2,1,0:T(8,128)(2,1)S(1)} %copy-done.15), kind=kOutput, calls=%fused_computation.20 | convolution fusion | flops 7247757312 | bytes 19660800 | tf_op jit(solution)/shard_map/dot_general | solution.py:15
  152.9 3.2 fusion.4
  156.8 3.5 %multiply_convert_fusion.1 = bf16[32,72,1024]{2,1,0:T(8,128)(2,1)S(1)} fusion(bf16[32,72,3200]{2,1,0:T(8,128)(2,1)} %convolution_convert_fusion.1, f32[32,72]{1,0:T(8,128)S(1)} %select_reduce_fusion), kind=kLoop, calls=%fused_computation.8 | loop fusion | flops 7077888 | bytes 9446400 | tf_op jit(solution)/shard_map/convert_element_type | solution.py:121
  162.5 3.8 %fusion.24 = f32[2304,384]{0,1:T(8,128)} fusion(bf16[2304,1024]{1,0:T(8,128)(2,1)S(1)} %bitcast.47, bf16[384,2048]{1,0:T(8,128)(2,1)S(1)} %bitcast.52), kind=kOutput, calls=%fused_computation.46 | convolution fusion | flops 1811939328 | bytes 9043968 | tf_op jit(solution)/shard_map/dot_general | solution.py:23
  166.3 4.9 %multiply_convert_fusion = bf16[32,72,1024]{2,1,0:T(8,128)(2,1)S(1)} fusion(f32[32,72]{1,0:T(8,128)} %copy-done.16, bf16[32,128,1024]{2,1,0:T(8,128)(2,1)} %bitcast.46, f32[32,128]{1,0:T(8,128)S(1)} %fusion.33, pred[32,128]{1,0:T(8,128)(4,1)} %copy-done.17), kind=kOutput, calls=%fused_computation.7 | convolution fusion | flops 614006784 | bytes 13136896 | tf_op jit(solution)/shard_map/srt,stc->src/dot_general | solution.py:116
  174.7 11.2 %convolution_convert_fusion.2 = bf16[2304,2048]{1,0:T(8,128)(2,1)S(1)} fusion(bf16[1,2048,768]{2,1,0:T(8,128)(2,1)} %param.14, bf16[2304,384]{0,1:T(8,128)(2,1)S(1)} %get-tuple-element.33, bf16[2304,384]{0,1:T(8,128)(2,1)S(1)} %get-tuple-element.32), kind=kOutput, calls=%fused_computation.2 | convolution fusion | flops 7259553792 | bytes 16121856 | tf_op jit(solution)/shard_map/dot_general | solution.py:42
  185.9 8.2 %convolution_convert_fusion = bf16[32,128,2048]{2,1,0:T(8,128)(2,1)} fusion(bf16[32,72,2048]{2,1,0:T(8,128)(2,1)S(1)} %bitcast.42, f32[32,128]{1,0:T(8,128)S(1)} %fusion.33, pred[32,128]{1,0:T(8,128)(4,1)S(1)} %copy-done.19), kind=kOutput, calls=%fused_computation | convolution fusion | flops 1216937984 | bytes 26234880 | tf_op jit(solution)/shard_map/srt,src->stc/dot_general | solution.py:130
  195.6 7.6 %fusion.8 = bf16[384,2048]{1,0:T(8,128)(2,1)S(1)} fusion(bf16[2304,384]{0,1:T(8,128)(2,1)S(1)} %copy-done.8, bf16[2304,1024]{1,0:T(8,128)(2,1)} %bitcast.39, bf16[2304,1024]{1,0:T(8,128)(2,1)} %bitcast.48), kind=kOutput, calls=%fused_computation.23 | convolution fusion | flops 3643539456 | bytes 12779520 | tf_op jit(solution)/shard_map/dot_general | solution.py:38
  204.5 3.8 %all-to-all-start = ((bf16[384,4,512]{2,0,1:T(8,128)(2,1)}), bf16[384,4,512]{2,0,1:T(8,128)(2,1)S(1)}, u32[]{:S(2)}, u32[]{:S(2)}) async-start(bf16[384,4,512]{2,0,1:T(8,128)(2,1)} %bitcast.36), calls=%async_computation.1 | async-start | bytes 3145728 | tf_op jit(solution)/shard_map/all_to_all | solution.py:153
  208.3 12.5 %convolution_convert_fusion.3 = bf16[2048,768]{1,0:T(8,128)(2,1)} fusion(bf16[2304,2048]{1,0:T(8,128)(2,1)} %bitcast.45, bf16[2304,384]{0,1:T(8,128)(2,1)} %copy-done.6, bf16[2304,384]{0,1:T(8,128)(2,1)S(1)} %copy-done.5), kind=kOutput, calls=%fused_computation.18 | convolution fusion | flops 7256408064 | bytes 16121856 | tf_op jit(solution)/shard_map/dot_general | solution.py:41
  220.8 7.9 %all-to-all-done = bf16[384,4,512]{2,0,1:T(8,128)(2,1)S(1)} async-done(((bf16[384,4,512]{2,0,1:T(8,128)(2,1)}), bf16[384,4,512]{2,0,1:T(8,128)(2,1)S(1)}, u32[]{:S(2)}, u32[]{:S(2)}) %all-to-all-start) | async-done | bytes 1572896 | tf_op jit(solution)/shard_map/all_to_all | solution.py:153
  229.8 3.8 %all-to-all-start.1 = ((bf16[4,512,768]{2,1,0:T(8,128)(2,1)}), bf16[4,512,768]{2,1,0:T(8,128)(2,1)S(1)}, u32[]{:S(2)}, u32[]{:S(2)}) async-start(bf16[4,512,768]{2,1,0:T(8,128)(2,1)} %bitcast.49), calls=%async_computation.2 | async-start | bytes 6291456 | tf_op jit(solution)/shard_map/all_to_all | solution.py:146
  233.7 2.7 convert_reduce_fusion.1
  236.4 33.5 %all-to-all-done.1 = bf16[4,512,768]{2,1,0:T(8,128)(2,1)S(1)} async-done(((bf16[4,512,768]{2,1,0:T(8,128)(2,1)}), bf16[4,512,768]{2,1,0:T(8,128)(2,1)S(1)}, u32[]{:S(2)}, u32[]{:S(2)}) %all-to-all-start.1) | async-done | bytes 3145760 | tf_op jit(solution)/shard_map/all_to_all | solution.py:146
  271.9 3.9 %fusion.26 = (bf16[512,768]{1,0:T(8,128)(2,1)S(1)}, f32[1,512,768]{2,1,0:T(8,128)}, f32[1,512,768]{2,1,0:T(8,128)}) fusion(bf16[1,2048,768]{2,1,0:T(8,128)(2,1)} %param.14, s32[]{:T(128)S(6)} %select_n.14, f32[512,768]{1,0:T(8,128)S(1)} %convert_reduce_fusion, f32[1,512,768]{2,1,0:T(8,128)S(1)} %copy-done.9, f32[1,512,768]{2,1,0:T(8,128)S(1)} %copy-done.10), kind=kLoop, calls=%fused_computation.50 | loop fusion | flops 5111808 | bytes 9437188 | tf_op jit(solution)/shard_map/broadcast_in_dim | solution.py:171
  277.6 3.7 %all-to-all-start.2 = ((bf16[4,512,768]{2,1,0:T(8,128)(2,1)}), bf16[4,512,768]{2,1,0:T(8,128)(2,1)S(1)}, u32[]{:S(2)}, u32[]{:S(2)}) async-start(bf16[4,512,768]{2,1,0:T(8,128)(2,1)} %broadcast_in_dim.40), calls=%async_computation.3 | async-start | bytes 6291456 | tf_op jit(solution)/shard_map/all_to_all | solution.py:170
  281.4 25.4 %reduce-scatter.2.cloned.1.call-done = bf16[128,2048]{1,0:T(8,128)(2,1)} async-done(((bf16[4096,2048]{1,0:T(8,128)(2,1)}), bf16[128,2048]{1,0:T(8,128)(2,1)}) %reduce-scatter.2.cloned.1.call-update) | async-done | bytes 524304 | tf_op jit(solution)/shard_map/reduce_scatter | solution.py:136
  306.8 3.4 subtract_convert_fusion.1
  310.2 6.5 %all-to-all-done.2 = bf16[4,512,768]{2,1,0:T(8,128)(2,1)S(1)} async-done(((bf16[4,512,768]{2,1,0:T(8,128)(2,1)}), bf16[4,512,768]{2,1,0:T(8,128)(2,1)S(1)}, u32[]{:S(2)}, u32[]{:S(2)}) %all-to-all-start.2) | async-done | bytes 3145760 | tf_op jit(solution)/shard_map/all_to_all | solution.py:170
  316.7 20.5 %all-gather.6.cloned.1.call-done = bf16[1,384,2048]{2,1,0:T(8,128)(2,1)} async-done(((bf16[1,384,512]{2,1,0:T(8,128)(2,1)}), bf16[1,384,2048]{2,1,0:T(8,128)(2,1)}) %all-gather.6.cloned.1.call-update) | async-done | bytes 1572880 | tf_op jit(solution)/shard_map/all_gather | solution.py:173
  (69 shorter events, 25.8 us)
Async XLA Ops:
  7.2 103.3 %copy-start.14 = (bf16[128,2048]{1,0:T(8,128)(2,1)S(1)}, bf16[128,2048]{1,0:T(8,128)(2,1)}, u32[]{:S(2)}) copy-start(bf16[128,2048]{1,0:T(8,128)(2,1)} %param.11) | copy-start | bytes 1572868
  7.2 103.3 %all-gather.8.cloned.1.call-start = ((), (), s32[]{:S(2)}) async-start(), calls=%async_computation.6 | async-start | bytes 27033600 | tf_op jit(solution)/shard_map/all_gather | solution.py:91
  11.8 154.5 %all-gather.10.cloned.1.call-start = ((), (), s32[]{:S(2)}) async-start(), calls=%async_computation.7 | async-start | bytes 8650752 | tf_op jit(solution)/shard_map/all_gather | solution.py:95
  111.2 195.6 %reduce-scatter.2.cloned.1.call-start = ((), (), s32[]{:S(2)}) async-start(), calls=%async_computation.4 | async-start | bytes 17301504 | tf_op jit(solution)/shard_map/reduce_scatter | solution.py:136
  132.8 9.4 %copy-start.15 = (bf16[1,2048,768]{2,1,0:T(8,128)(2,1)S(1)}, bf16[1,2048,768]{2,1,0:T(8,128)(2,1)}, u32[]{:S(2)}) copy-start(bf16[1,2048,768]{2,1,0:T(8,128)(2,1)} %param.14) | copy-start | bytes 9437188
  152.8 3.2 copy-start.18
  152.9 3.2 copy-start.20
  156.8 3.6 %copy-start.16 = (f32[32,72]{1,0:T(8,128)}, f32[32,72]{1,0:T(8,128)S(1)}, u32[]{:S(2)}) copy-start(f32[32,72]{1,0:T(8,128)S(1)} %select_reduce_fusion) | copy-start | bytes 27652
  156.8 5.8 %copy-start.12 = (bf16[1,384,2048]{2,1,0:T(8,128)(2,1)S(1)}, bf16[1,384,2048]{2,1,0:T(8,128)(2,1)}, u32[]{:S(2)}) copy-start(bf16[1,384,2048]{2,1,0:T(8,128)(2,1)} %param.15) | copy-start | bytes 4718596
  160.3 2.2 copy-start.7
  166.3 5.0 %copy-start.1 = (f32[2304,384]{0,1:T(8,128)S(1)}, f32[2304,384]{0,1:T(8,128)}, u32[]{:S(2)}) copy-start(f32[2304,384]{0,1:T(8,128)} %get-tuple-element.16) | copy-start | bytes 10616836
  166.3 5.5 %copy-start.2 = (f32[2304,384]{0,1:T(8,128)S(1)}, f32[2304,384]{0,1:T(8,128)}, u32[]{:S(2)}) copy-start(f32[2304,384]{0,1:T(8,128)} %fusion.24) | copy-start | bytes 10616836
  166.3 5.9 %copy-start.13 = (bf16[1,384,2048]{2,1,0:T(8,128)(2,1)S(1)}, bf16[1,384,2048]{2,1,0:T(8,128)(2,1)}, u32[]{:S(2)}) copy-start(bf16[1,384,2048]{2,1,0:T(8,128)(2,1)} %param.15) | copy-start | bytes 4718596
  171.3 3.4 copy-start
  174.6 11.2 %copy-start.4 = (bf16[2304,384]{0,1:T(8,128)(2,1)}, bf16[2304,384]{0,1:T(8,128)(2,1)S(1)}, u32[]{:S(2)}) copy-start(bf16[2304,384]{0,1:T(8,128)(2,1)S(1)} %get-tuple-element.32) | copy-start | bytes 5308420
  174.6 11.2 %copy-start.6 = (bf16[2304,384]{0,1:T(8,128)(2,1)}, bf16[2304,384]{0,1:T(8,128)(2,1)S(1)}, u32[]{:S(2)}) copy-start(bf16[2304,384]{0,1:T(8,128)(2,1)S(1)} %get-tuple-element.33) | copy-start | bytes 5308420
  174.7 11.2 %copy-start.19 = (pred[32,128]{1,0:T(8,128)(4,1)S(1)}, pred[32,128]{1,0:T(8,128)(4,1)}, u32[]{:S(2)}) copy-start(pred[32,128]{1,0:T(8,128)(4,1)} %copy-done.17) | copy-start | bytes 12292
  203.2 5.2 %copy-start.5 = (bf16[2304,384]{0,1:T(8,128)(2,1)S(1)}, bf16[2304,384]{0,1:T(8,128)(2,1)}, u32[]{:S(2)}) copy-start(bf16[2304,384]{0,1:T(8,128)(2,1)} %copy-done.4) | copy-start | bytes 5308420
  204.5 24.2 %all-to-all-start = ((bf16[384,4,512]{2,0,1:T(8,128)(2,1)}), bf16[384,4,512]{2,0,1:T(8,128)(2,1)S(1)}, u32[]{:S(2)}, u32[]{:S(2)}) async-start(bf16[384,4,512]{2,0,1:T(8,128)(2,1)} %bitcast.36), calls=%async_computation.1 | async-start | bytes 3145728 | tf_op jit(solution)/shard_map/all_to_all | solution.py:153
  229.8 40.1 %all-to-all-start.1 = ((bf16[4,512,768]{2,1,0:T(8,128)(2,1)}), bf16[4,512,768]{2,1,0:T(8,128)(2,1)S(1)}, u32[]{:S(2)}, u32[]{:S(2)}) async-start(bf16[4,512,768]{2,1,0:T(8,128)(2,1)} %bitcast.49), calls=%async_computation.2 | async-start | bytes 6291456 | tf_op jit(solution)/shard_map/all_to_all | solution.py:146
  269.9 2.0 copy-start.10
  277.6 39.1 %all-to-all-start.2 = ((bf16[4,512,768]{2,1,0:T(8,128)(2,1)}), bf16[4,512,768]{2,1,0:T(8,128)(2,1)S(1)}, u32[]{:S(2)}, u32[]{:S(2)}) async-start(bf16[4,512,768]{2,1,0:T(8,128)(2,1)} %broadcast_in_dim.40), calls=%async_computation.3 | async-start | bytes 6291456 | tf_op jit(solution)/shard_map/all_to_all | solution.py:170
  281.3 55.9 %all-gather.6.cloned.1.call-start = ((), (), s32[]{:S(2)}) async-start(), calls=%async_computation.5 | async-start | bytes 1966080 | tf_op jit(solution)/shard_map/all_gather | solution.py:173
  337.2 2.5 copy-start.11
  (4 other events, 4.7 us)
Sparse Core Ops, SparseCore 0:
  11.9 98.4 all-gather.7
  113.3 52.3 all-gather.9
  194.2 112.5 reduce-scatter.1
  310.4 26.8 all-gather.5
where the time goes:
time: 348 us; the launch traced here: 347 us
  waiting for transfers between devices  193 us (55%)
  matrix products  77.2 us (22%)
  other arithmetic  26.3 us (8%)
  local copies, waits for them, and re-layouts  25.9 us (7%)
  between operations  14 us (4%)
  starting transfers between devices  11.5 us (3%)
    all_gather x1, waiting for transfers between devices, local(): lax.all_gather(jnp.concatenate([tokens, cotangent[:, :half_width], meta],...  98.6 us
    all_to_all x1, waiting for transfers between devices, local(): lax.all_to_all(grad_pair.astype(jnp.bfloat16).reshape(groups, share_rows,...  33.5 us
    reduce_scatter x1, waiting for transfers between devices, local(): lax.psum_scatter(dense.reshape(expert_count * local_tokens, model_width),...  25.4 us
    all_gather x1, waiting for transfers between devices, local(): full_down = lax.all_gather(new_down, 'group', axis=2, tiled=True)  20.5 us
    dot_general x1, matrix products, local(): jnp.einsum('srt,stc->src', pick_b, first, preferred_element_type=jnp.floa...  15.9 us
    dot_general x1, matrix products, expert_backward(): jnp.dot(inputs.T, pair_grad, preferred_element_type=jnp.float32)  12.5 us
    unnamed x45, local copies, waits for them, and re-layouts  11.6 us
    dot_general x1, matrix products, expert_backward(): jnp.dot(pair_grad, weight_gate_up.T, preferred_element_type=jnp.float32)  11.2 us
  transfers between devices with their start and end apart: 7, of which 6 were waited for; matrix products, arithmetic and copies ran while one was open for 25% of the time, Pallas kernels for 0%

commit v1 on v0

--- a/solution.py
+++ b/solution.py
@@ -170,7 +170,9 @@
     full_pair = lax.all_to_all(
         jnp.broadcast_to(new_pair, (groups, share_rows, pair_width)), "group", 0, 0, tiled=True
     ).reshape(1, model_width, pair_width)
-    full_down = lax.all_gather(new_down, "group", axis=2, tiled=True)
+    full_down = jnp.concatenate(
+        lax.all_to_all(jnp.stack([new_down] * lax.axis_size("group")), "group", 0, 0), axis=2
+    )
     return (token_grad, full_pair, full_down, first_pair, second_pair, first_down, second_down)
 
 

time: 348 us -> 353 us (1.014)
  waiting for transfers between devices: 193 us -> 186 us
  starting transfers between devices: 11.5 us -> 16.4 us
  local copies, waits for them, and re-layouts: 25.9 us -> 29.7 us
    all_gather x1 -> x0, waiting for transfers between devices: 20.5 us -> none  [local(): full_down = lax.all_gather(new_down, 'group', axis=2, tiled=True)]
    all_to_all x0 -> x1, waiting for transfers between devices: none -> 17.7 us  [local(): lax.all_to_all(jnp.stack([new_down] * lax.axis_size('group')), 'group', 0...]
    all_to_all x1, waiting for transfers between devices: 33.5 us -> 26.8 us  [local(): lax.all_to_all(grad_pair.astype(jnp.bfloat16).reshape(groups, share_rows,...]
    all_to_all x1, waiting for transfers between devices: 7.91 us -> 13.7 us  [local(): lax.all_to_all(grad_down.astype(jnp.bfloat16).reshape(hidden_count, group...]
    all_to_all x0 -> x1, starting transfers between devices: none -> 4.35 us  [local(): lax.all_to_all(jnp.stack([new_down] * lax.axis_size('group')), 'group', 0...]
    unnamed x45 -> x41, local copies, waits for them, and re-layouts: 11.6 us -> 11.5 us
where the time goes in v1:
time: 353 us; the launch traced here: 350 us
  waiting for transfers between devices  186 us (53%)
  matrix products  77.5 us (22%)
  local copies, waits for them, and re-layouts  29.7 us (8%)
  other arithmetic  26.1 us (7%)
  starting transfers between devices  16.4 us (5%)
  between operations  14 us (4%)
    all_gather x1, waiting for transfers between devices, local(): lax.all_gather(jnp.concatenate([tokens, cotangent[:, :half_width], meta],...  98.6 us
    all_to_all x1, waiting for transfers between devices, local(): lax.all_to_all(grad_pair.astype(jnp.bfloat16).reshape(groups, share_rows,...  26.8 us
    reduce_scatter x1, waiting for transfers between devices, local(): lax.psum_scatter(dense.reshape(expert_count * local_tokens, model_width),...  26.2 us
    all_to_all x1, waiting for transfers between devices, local(): lax.all_to_all(jnp.stack([new_down] * lax.axis_size('group')), 'group', 0...  17.7 us
    dot_general x1, matrix products, local(): jnp.einsum('srt,stc->src', pick_b, first, preferred_element_type=jnp.floa...  15.9 us
    all_to_all x1, waiting for transfers between devices, local(): lax.all_to_all(grad_down.astype(jnp.bfloat16).reshape(hidden_count, group...  13.7 us
    unnamed x41, local copies, waits for them, and re-layouts  11.5 us
    dot_general x1, matrix products, expert_backward(): jnp.dot(inputs.T, pair_grad, preferred_element_type=jnp.float32)  11.2 us
  transfers between devices with their start and end apart: 7, of which 6 were waited for; matrix products, arithmetic and copies ran while one was open for 25% of the time, Pallas kernels for 0%

profile of v1, /device:TPU:1, one launch (start us, length us, event | category | flops | bytes accessed | tf_op | source)
XLA Modules:
  0.0 350.0 jit_solution(2214300360844579427)
XLA Ops:
  11.8 98.6 %all-gather.5.cloned.1.call-done = bf16[4096,3200]{1,0:T(8,128)(2,1)} async-done(((bf16[128,3200]{1,0:T(8,128)(2,1)}), bf16[4096,3200]{1,0:T(8,128)(2,1)}) %all-gather.5.cloned.1.call-update) | async-done | bytes 26214416 | tf_op jit(solution)/shard_map/all_gather | solution.py:91
  112.7 3.0 fusion.12
  116.9 15.9 %convolution_convert_fusion.1 = bf16[32,72,3200]{2,1,0:T(8,128)(2,1)} fusion(bf16[32,128,3200]{2,1,0:T(8,128)(2,1)} %bitcast.46, f32[32,128]{1,0:T(8,128)S(1)} %fusion.34, pred[32,128]{1,0:T(8,128)(4,1)S(1)} %convert_compare_fusion), kind=kOutput, calls=%fused_computation.1 | convolution fusion | flops 1895399424 | bytes 40980480 | tf_op jit(solution)/shard_map/srt,stc->src/dot_general | solution.py:111
  132.8 9.4 %slice.59 = bf16[32,72,2048]{2,1,0:T(8,128)(2,1)} slice(bf16[32,72,3200]{2,1,0:T(8,128)(2,1)} %convolution_convert_fusion.1), slice={[0:32], [0:72], [0:2048]} | slice | bytes 18874368 | tf_op jit(solution)/shard_map/slice | solution.py:114
  142.3 10.6 %fusion.6 = f32[2304,768]{0,1:T(8,128)S(1)} fusion(bf16[2304,2048]{1,0:T(8,128)(2,1)} %bitcast.49, bf16[1,2048,768]{2,1,0:T(8,128)(2,1)S(1)} %copy-done.13), kind=kOutput, calls=%fused_computation.20 | convolution fusion | flops 7247757312 | bytes 19660800 | tf_op jit(solution)/shard_map/dot_general | solution.py:15
  152.9 3.2 fusion.4
  156.8 3.5 %multiply_convert_fusion.1 = bf16[32,72,1024]{2,1,0:T(8,128)(2,1)S(1)} fusion(bf16[32,72,3200]{2,1,0:T(8,128)(2,1)} %convolution_convert_fusion.1, f32[32,72]{1,0:T(8,128)S(1)} %select_reduce_fusion), kind=kLoop, calls=%fused_computation.8 | loop fusion | flops 7077888 | bytes 9446400 | tf_op jit(solution)/shard_map/convert_element_type | solution.py:121
  162.6 3.8 %fusion.24 = f32[2304,384]{0,1:T(8,128)} fusion(bf16[2304,1024]{1,0:T(8,128)(2,1)S(1)} %bitcast.54, bf16[384,2048]{1,0:T(8,128)(2,1)S(1)} %bitcast.59), kind=kOutput, calls=%fused_computation.46 | convolution fusion | flops 1811939328 | bytes 9043968 | tf_op jit(solution)/shard_map/dot_general | solution.py:23
  166.3 4.9 %multiply_convert_fusion = bf16[32,72,1024]{2,1,0:T(8,128)(2,1)S(1)} fusion(f32[32,72]{1,0:T(8,128)} %copy-done.14, bf16[32,128,1024]{2,1,0:T(8,128)(2,1)} %bitcast.51, f32[32,128]{1,0:T(8,128)S(1)} %fusion.34, pred[32,128]{1,0:T(8,128)(4,1)} %copy-done.15), kind=kOutput, calls=%fused_computation.7 | convolution fusion | flops 614006784 | bytes 13136896 | tf_op jit(solution)/shard_map/srt,stc->src/dot_general | solution.py:116
  174.7 11.2 %convolution_convert_fusion.2 = bf16[2304,2048]{1,0:T(8,128)(2,1)S(1)} fusion(bf16[1,2048,768]{2,1,0:T(8,128)(2,1)} %param.14, bf16[2304,384]{0,1:T(8,128)(2,1)S(1)} %get-tuple-element.40, bf16[2304,384]{0,1:T(8,128)(2,1)S(1)} %get-tuple-element.39), kind=kOutput, calls=%fused_computation.2 | convolution fusion | flops 7259553792 | bytes 16121856 | tf_op jit(solution)/shard_map/dot_general | solution.py:42
  185.9 8.2 %convolution_convert_fusion = bf16[32,128,2048]{2,1,0:T(8,128)(2,1)} fusion(bf16[32,72,2048]{2,1,0:T(8,128)(2,1)S(1)} %bitcast.47, f32[32,128]{1,0:T(8,128)S(1)} %fusion.34, pred[32,128]{1,0:T(8,128)(4,1)S(1)} %copy-done.17), kind=kOutput, calls=%fused_computation | convolution fusion | flops 1216937984 | bytes 26234880 | tf_op jit(solution)/shard_map/srt,src->stc/dot_general | solution.py:130
  196.1 11.2 %convolution_convert_fusion.3 = bf16[2048,768]{1,0:T(8,128)(2,1)} fusion(bf16[2304,2048]{1,0:T(8,128)(2,1)} %bitcast.50, bf16[2304,384]{0,1:T(8,128)(2,1)S(1)} %copy-done.6, bf16[2304,384]{0,1:T(8,128)(2,1)S(1)} %copy-done.4), kind=kOutput, calls=%fused_computation.18 | convolution fusion | flops 7256408064 | bytes 16121856 | tf_op jit(solution)/shard_map/dot_general | solution.py:41
  207.4 3.9 %all-to-all-start.1 = ((bf16[4,512,768]{2,1,0:T(8,128)(2,1)}), bf16[4,512,768]{2,1,0:T(8,128)(2,1)S(1)}, u32[]{:S(2)}, u32[]{:S(2)}) async-start(bf16[4,512,768]{2,1,0:T(8,128)(2,1)} %bitcast.56), calls=%async_computation.2 | async-start | bytes 6291456 | tf_op jit(solution)/shard_map/all_to_all | solution.py:146
  211.2 9.1 %fusion.8 = bf16[384,2048]{1,0:T(8,128)(2,1)S(1)} fusion(bf16[2304,384]{0,1:T(8,128)(2,1)} %get-tuple-element.18, bf16[2304,1024]{1,0:T(8,128)(2,1)} %bitcast.44, bf16[2304,1024]{1,0:T(8,128)(2,1)} %bitcast.55), kind=kOutput, calls=%fused_computation.23 | convolution fusion | flops 3643539456 | bytes 12779520 | tf_op jit(solution)/shard_map/dot_general | solution.py:38
  221.7 26.8 %all-to-all-done.1 = bf16[4,512,768]{2,1,0:T(8,128)(2,1)S(1)} async-done(((bf16[4,512,768]{2,1,0:T(8,128)(2,1)}), bf16[4,512,768]{2,1,0:T(8,128)(2,1)S(1)}, u32[]{:S(2)}, u32[]{:S(2)}) %all-to-all-start.1) | async-done | bytes 3145760 | tf_op jit(solution)/shard_map/all_to_all | solution.py:146
  248.5 4.4 %all-to-all-start = ((bf16[384,4,512]{2,0,1:T(8,128)(2,1)}), bf16[384,4,512]{2,0,1:T(8,128)(2,1)}, u32[]{:S(2)}, u32[]{:S(2)}) async-start(bf16[384,4,512]{2,0,1:T(8,128)(2,1)} %bitcast.52), calls=%async_computation.1 | async-start | bytes 3145728 | tf_op jit(solution)/shard_map/all_to_all | solution.py:153
  254.8 3.9 %fusion.26 = (bf16[512,768]{1,0:T(8,128)(2,1)S(1)}, f32[1,512,768]{2,1,0:T(8,128)}, f32[1,512,768]{2,1,0:T(8,128)}) fusion(bf16[1,2048,768]{2,1,0:T(8,128)(2,1)} %param.14, s32[]{:T(128)S(6)} %select_n.14, f32[512,768]{1,0:T(8,128)S(1)} %convert_reduce_fusion, f32[1,512,768]{2,1,0:T(8,128)S(1)} %copy-done.8, f32[1,512,768]{2,1,0:T(8,128)S(1)} %copy-done.9), kind=kLoop, calls=%fused_computation.50 | loop fusion | flops 5111808 | bytes 9437188 | tf_op jit(solution)/shard_map/broadcast_in_dim | solution.py:171
  258.7 13.7 %all-to-all-done = bf16[384,4,512]{2,0,1:T(8,128)(2,1)} async-done(((bf16[384,4,512]{2,0,1:T(8,128)(2,1)}), bf16[384,4,512]{2,0,1:T(8,128)(2,1)}, u32[]{:S(2)}, u32[]{:S(2)}) %all-to-all-start) | async-done | bytes 1572896 | tf_op jit(solution)/shard_map/all_to_all | solution.py:153
  274.2 3.7 %all-to-all-start.2 = ((bf16[4,512,768]{2,1,0:T(8,128)(2,1)}), bf16[4,512,768]{2,1,0:T(8,128)(2,1)S(1)}, u32[]{:S(2)}, u32[]{:S(2)}) async-start(bf16[4,512,768]{2,1,0:T(8,128)(2,1)} %broadcast_in_dim.40), calls=%async_computation.3 | async-start | bytes 6291456 | tf_op jit(solution)/shard_map/all_to_all | solution.py:170
  280.6 26.2 %reduce-scatter.2.cloned.1.call-done = bf16[128,2048]{1,0:T(8,128)(2,1)} async-done(((bf16[4096,2048]{1,0:T(8,128)(2,1)}), bf16[128,2048]{1,0:T(8,128)(2,1)}) %reduce-scatter.2.cloned.1.call-update) | async-done | bytes 524304 | tf_op jit(solution)/shard_map/reduce_scatter | solution.py:136
  306.8 3.4 fusion.33
  310.2 3.2 all-to-all-done.2
  314.6 4.3 %all-to-all-start.3 = ((bf16[4,1,384,512]{3,2,1,0:T(8,128)(2,1)}), bf16[4,1,384,512]{3,2,1,0:T(8,128)(2,1)}, u32[]{:S(2)}, u32[]{:S(2)}) async-start(bf16[4,1,384,512]{3,2,1,0:T(8,128)(2,1)} %stack.2), calls=%async_computation.4 | async-start | bytes 3145728 | tf_op jit(solution)/shard_map/all_to_all | solution.py:174
  319.0 17.7 %all-to-all-done.3 = bf16[4,1,384,512]{3,2,1,0:T(8,128)(2,1)} async-done(((bf16[4,1,384,512]{3,2,1,0:T(8,128)(2,1)}), bf16[4,1,384,512]{3,2,1,0:T(8,128)(2,1)}, u32[]{:S(2)}, u32[]{:S(2)}) %all-to-all-start.3) | async-done | bytes 1572896 | tf_op jit(solution)/shard_map/all_to_all | solution.py:174
  (66 shorter events, 32.1 us)
Async XLA Ops:
  7.2 103.3 %copy-start.12 = (bf16[128,2048]{1,0:T(8,128)(2,1)S(1)}, bf16[128,2048]{1,0:T(8,128)(2,1)}, u32[]{:S(2)}) copy-start(bf16[128,2048]{1,0:T(8,128)(2,1)} %param.11) | copy-start | bytes 1572868
  7.2 103.3 %all-gather.5.cloned.1.call-start = ((), (), s32[]{:S(2)}) async-start(), calls=%async_computation.6 | async-start | bytes 27033600 | tf_op jit(solution)/shard_map/all_gather | solution.py:91
  11.8 154.6 %all-gather.7.cloned.1.call-start = ((), (), s32[]{:S(2)}) async-start(), calls=%async_computation.7 | async-start | bytes 8650752 | tf_op jit(solution)/shard_map/all_gather | solution.py:95
  111.2 195.6 %reduce-scatter.2.cloned.1.call-start = ((), (), s32[]{:S(2)}) async-start(), calls=%async_computation.5 | async-start | bytes 17301504 | tf_op jit(solution)/shard_map/reduce_scatter | solution.py:136
  132.8 9.4 %copy-start.13 = (bf16[1,2048,768]{2,1,0:T(8,128)(2,1)S(1)}, bf16[1,2048,768]{2,1,0:T(8,128)(2,1)}, u32[]{:S(2)}) copy-start(bf16[1,2048,768]{2,1,0:T(8,128)(2,1)} %param.14) | copy-start | bytes 9437188
  152.9 3.3 copy-start.16
  152.9 3.2 copy-start.18
  156.8 3.5 %copy-start.14 = (f32[32,72]{1,0:T(8,128)}, f32[32,72]{1,0:T(8,128)S(1)}, u32[]{:S(2)}) copy-start(f32[32,72]{1,0:T(8,128)S(1)} %select_reduce_fusion) | copy-start | bytes 27652
  156.8 5.8 %copy-start.10 = (bf16[1,384,2048]{2,1,0:T(8,128)(2,1)S(1)}, bf16[1,384,2048]{2,1,0:T(8,128)(2,1)}, u32[]{:S(2)}) copy-start(bf16[1,384,2048]{2,1,0:T(8,128)(2,1)} %param.15) | copy-start | bytes 4718596
  160.3 2.2 copy-start.7
  166.3 5.0 %copy-start.1 = (f32[2304,384]{0,1:T(8,128)S(1)}, f32[2304,384]{0,1:T(8,128)}, u32[]{:S(2)}) copy-start(f32[2304,384]{0,1:T(8,128)} %get-tuple-element.16) | copy-start | bytes 10616836
  166.3 5.5 %copy-start.2 = (f32[2304,384]{0,1:T(8,128)S(1)}, f32[2304,384]{0,1:T(8,128)}, u32[]{:S(2)}) copy-start(f32[2304,384]{0,1:T(8,128)} %fusion.24) | copy-start | bytes 10616836
  166.3 5.9 %copy-start.11 = (bf16[1,384,2048]{2,1,0:T(8,128)(2,1)S(1)}, bf16[1,384,2048]{2,1,0:T(8,128)(2,1)}, u32[]{:S(2)}) copy-start(bf16[1,384,2048]{2,1,0:T(8,128)(2,1)} %param.15) | copy-start | bytes 4718596
  171.3 3.4 copy-start
  174.7 11.2 %copy-start.3 = (bf16[2304,384]{0,1:T(8,128)(2,1)}, bf16[2304,384]{0,1:T(8,128)(2,1)S(1)}, u32[]{:S(2)}) copy-start(bf16[2304,384]{0,1:T(8,128)(2,1)S(1)} %get-tuple-element.39) | copy-start | bytes 5308420
  174.7 11.2 %copy-start.5 = (bf16[2304,384]{0,1:T(8,128)(2,1)}, bf16[2304,384]{0,1:T(8,128)(2,1)S(1)}, u32[]{:S(2)}) copy-start(bf16[2304,384]{0,1:T(8,128)(2,1)S(1)} %get-tuple-element.40) | copy-start | bytes 5308420
  174.7 11.2 %copy-start.17 = (pred[32,128]{1,0:T(8,128)(4,1)S(1)}, pred[32,128]{1,0:T(8,128)(4,1)}, u32[]{:S(2)}) copy-start(pred[32,128]{1,0:T(8,128)(4,1)} %copy-done.15) | copy-start | bytes 12292
  194.1 1.5 copy-start.4
  194.1 2.0 copy-start.6
  207.4 41.1 %all-to-all-start.1 = ((bf16[4,512,768]{2,1,0:T(8,128)(2,1)}), bf16[4,512,768]{2,1,0:T(8,128)(2,1)S(1)}, u32[]{:S(2)}, u32[]{:S(2)}) async-start(bf16[4,512,768]{2,1,0:T(8,128)(2,1)} %bitcast.56), calls=%async_computation.2 | async-start | bytes 6291456 | tf_op jit(solution)/shard_map/all_to_all | solution.py:146
  248.5 23.9 %all-to-all-start = ((bf16[384,4,512]{2,0,1:T(8,128)(2,1)}), bf16[384,4,512]{2,0,1:T(8,128)(2,1)}, u32[]{:S(2)}, u32[]{:S(2)}) async-start(bf16[384,4,512]{2,0,1:T(8,128)(2,1)} %bitcast.52), calls=%async_computation.1 | async-start | bytes 3145728 | tf_op jit(solution)/shard_map/all_to_all | solution.py:153
  252.9 1.9 copy-start.9
  274.2 39.1 %all-to-all-start.2 = ((bf16[4,512,768]{2,1,0:T(8,128)(2,1)}), bf16[4,512,768]{2,1,0:T(8,128)(2,1)S(1)}, u32[]{:S(2)}, u32[]{:S(2)}) async-start(bf16[4,512,768]{2,1,0:T(8,128)(2,1)} %broadcast_in_dim.40), calls=%async_computation.3 | async-start | bytes 6291456 | tf_op jit(solution)/shard_map/all_to_all | solution.py:170
  314.6 22.1 %all-to-all-start.3 = ((bf16[4,1,384,512]{3,2,1,0:T(8,128)(2,1)}), bf16[4,1,384,512]{3,2,1,0:T(8,128)(2,1)}, u32[]{:S(2)}, u32[]{:S(2)}) async-start(bf16[4,1,384,512]{3,2,1,0:T(8,128)(2,1)} %stack.2), calls=%async_computation.4 | async-start | bytes 3145728 | tf_op jit(solution)/shard_map/all_to_all | solution.py:174
  (2 other events, 2.0 us)
Sparse Core Ops, SparseCore 0:
  11.9 98.4 all-gather.4
  113.3 52.3 all-gather.6
  194.3 112.4 reduce-scatter.1
